TPU v7x, 32 devices: a whole 2x2x4 slice. The times are simulated.
32 devices in a mesh: rep: 2 (over y), grp: 4 (over z), sub: 4 (over x, core).
Axes of the slice: x: 2, y: 2, z: 4, core: 2. Of those that a mesh axis runs over, the one named last changes fastest.
Arguments:
- volume: bfloat16 [256, 8, 8, 128], P(None, ('rep', 'grp'), 'sub'), parts along dimension 1, may hold values from -6 to 6
- cotangent: bfloat16 [256, 8, 8, 128], P(None, ('rep', 'grp'), 'sub'), parts along dimension 1, may hold values from -6 to 6
- first_weight: bfloat16 [256, 256], replicated, may hold values from -0.375 to 0.375
- group_weight: bfloat16 [256, 8, 3, 3, 3], replicated, may hold values from -0.4375 to 0.4375
- third_weight: bfloat16 [256, 256], replicated, may hold values from -0.375 to 0.375
Outputs:
- block_output: bfloat16 [256, 8, 8, 128], P(None, ('rep', 'grp'), 'sub'), parts along dimension 1
- volume_grad: bfloat16 [256, 8, 8, 128], P(None, ('rep', 'grp'), 'sub'), parts along dimension 1
- first_grad: float32 [512, 256], P('rep'), parts along dimension 0
- group_grad: float32 [512, 8, 3, 3, 3], P(('rep', 'grp')), parts along dimension 0
- third_grad: float32 [512, 256], P('rep'), parts along dimension 0
There are 2 independent parts, one for each index of `rep`. A program takes and returns all parts, laid end to end along the dimension named above; an argument that names none is the same for every part. Nothing has to cross between parts.
All inputs are finite; a program needn't handle non-finite values.
Results may differ from a plain program's by a relative error of at most 0.0073.
Values may be sent and summed in bfloat16 or wider, within the bound.
No kernel may reach another device: no remote copies, remote signals or barrier semaphores. Data moves between devices by JAX's collectives and lax.ppermute only.
A program may use at most 64 MiB of HBM per device.

v0:
```python
import math
import jax
import jax.numpy as jnp
from jax import lax
from jax.sharding import PartitionSpec as P

GW = 8


def padded_2(block, sides, width):
    for axis, dim in sides:
        count = lax.axis_size(axis)
        forward = [(i, i + 1) for i in range(count - 1)]
        backward = [(target, source) for source, target in forward]
        low = lax.ppermute(
            lax.slice_in_dim(block, block.shape[dim] - width, None, axis=dim), axis, forward
        )
        high = lax.ppermute(lax.slice_in_dim(block, 0, width, axis=dim), axis, backward)
        block = jnp.concatenate([low, block, high], axis=dim)
    return block


def silu_slope(values):
    sigma = jax.nn.sigmoid(values)
    return sigma * (1.0 + values * (1.0 - sigma))


def dense_conv(source, kernel, depth_pad):
    padding = ((depth_pad, depth_pad), (0, 0), (1, 1))
    return lax.conv_general_dilated(
        source[None],
        kernel,
        (1, 1, 1),
        padding,
        dimension_numbers=("NCDHW", "OIDHW", "NCDHW"),
        preferred_element_type=jnp.float32,
    )[0]


def block_diagonal(kernel):
    rows = kernel.shape[0]
    tiled = jnp.tile(kernel, (1, rows // GW, 1, 1, 1))
    group_of = jnp.arange(rows) // GW
    mask = (group_of[:, None] == group_of[None, :]).astype(kernel.dtype)
    return tiled * mask[:, :, None, None, None]


def diagonal_blocks(dense):
    rows = dense.shape[1]
    groups = rows // GW
    shaped = dense.reshape(groups, GW, rows, *dense.shape[2:])
    group_of = jnp.arange(rows) // GW
    mask = (jnp.arange(groups)[:, None] == group_of[None, :]).astype(dense.dtype)
    picked = (shaped * mask[:, None, :, None, None, None]).sum(axis=0)
    return picked.transpose(1, 0, 2, 3, 4)


def weight_grad(padded, deltas):
    return lax.conv_general_dilated(
        padded[None],
        deltas[None],
        (1, 1, 1),
        "VALID",
        dimension_numbers=("CNDHW", "IODHW", "NCDHW"),
        preferred_element_type=jnp.float32,
    )


def per_device(volume, cotangent, first_weight, group_weight, third_weight):
    channels, depth, height, width = volume.shape
    flattened = volume.reshape(channels, -1)
    contract_lead = (((0,), (0,)), ((), ()))
    contract_tail = (((1,), (1,)), ((), ()))
    total_cells = depth * lax.axis_size("grp") * height * lax.axis_size("sub") * width
    factor = 1.0 / math.sqrt(total_cells)
    group_rows = channels // lax.axis_size("grp")
    first_pre = lax.dot_general(
        first_weight, flattened, contract_lead, preferred_element_type=jnp.float32
    )
    first_act = jax.nn.silu(first_pre).astype(jnp.bfloat16).reshape(volume.shape)
    own_kernel = lax.dynamic_slice_in_dim(
        group_weight, lax.axis_index("grp") * group_rows, group_rows, 0
    )
    dense_kernel = block_diagonal(own_kernel)
    gathered = lax.all_to_all(first_act, "grp", split_axis=0, concat_axis=1, tiled=True)
    padded_act = padded_2(gathered, (("sub", 2),), 1)
    group_pre = dense_conv(padded_act, dense_kernel, 1)
    group_act = jax.nn.silu(group_pre).astype(jnp.bfloat16)
    returned = lax.all_to_all(group_act, "grp", split_axis=1, concat_axis=0, tiled=True)
    act_flat = returned.reshape(channels, -1)
    summed = flattened.astype(jnp.float32) + lax.dot_general(
        third_weight, act_flat, contract_lead, preferred_element_type=jnp.float32
    )
    block_output = jax.nn.silu(summed).astype(jnp.bfloat16).reshape(volume.shape)
    third_delta = (cotangent.reshape(channels, -1).astype(jnp.float32) * silu_slope(summed)).astype(
        jnp.bfloat16
    )
    third_part = lax.dot_general(
        act_flat, third_delta, contract_tail, preferred_element_type=jnp.float32
    )
    third_grad = lax.psum(third_part, ("grp", "sub")) * factor
    hidden_grad = (
        jnp.dot(third_weight, third_delta, preferred_element_type=jnp.float32)
        .astype(jnp.bfloat16)
        .reshape(volume.shape)
    )
    arriving = lax.all_to_all(hidden_grad, "grp", split_axis=0, concat_axis=1, tiled=True)
    group_delta = (arriving.astype(jnp.float32) * silu_slope(group_pre)).astype(jnp.bfloat16)
    delta_rim = padded_2(group_delta, (("sub", 2),), 1)
    flipped = dense_kernel.transpose(1, 0, 2, 3, 4)[:, :, ::-1, ::-1, ::-1]
    inner_local = dense_conv(delta_rim, flipped, 1).astype(jnp.bfloat16)
    dense_grad = weight_grad(jnp.pad(padded_act, ((0, 0), (1, 1), (0, 0), (1, 1))), group_delta)
    kernel_part = diagonal_blocks(dense_grad)
    inner_grad = lax.all_to_all(inner_local, "grp", split_axis=1, concat_axis=0, tiled=True)
    group_grad = lax.psum(kernel_part, "sub") * factor
    first_delta = (
        inner_grad.reshape(channels, -1).astype(jnp.float32) * silu_slope(first_pre)
    ).astype(jnp.bfloat16)
    first_part = lax.dot_general(
        flattened, first_delta, contract_tail, preferred_element_type=jnp.float32
    )
    volume_grad = (
        (
            third_delta.astype(jnp.float32)
            + jnp.dot(first_weight, first_delta, preferred_element_type=jnp.float32)
        )
        .astype(jnp.bfloat16)
        .reshape(volume.shape)
    )
    first_grad = lax.psum(first_part, ("grp", "sub")) * factor
    return (block_output, volume_grad, first_grad, group_grad, third_grad)


def solution(mesh):
    in_specs = (
        P(None, ("rep", "grp"), "sub", None),
        P(None, ("rep", "grp"), "sub", None),
        P(),
        P(),
        P(),
    )
    out_specs = (
        P(None, ("rep", "grp"), "sub", None),
        P(None, ("rep", "grp"), "sub", None),
        P("rep", None),
        P(("rep", "grp"), None, None, None, None),
        P("rep", None),
    )
    return jax.shard_map(
        per_device, mesh=mesh, in_specs=in_specs, out_specs=out_specs, check_vma=False
    )
```

profile of v0, /device:TPU:1, one launch (start us, length us, event | category | flops | bytes accessed | tf_op | source)
XLA Modules:
  0.0 194.1 jit_solution(14904769792690059259)
XLA Ops:
  7.2 1.0 copy.70
  8.2 1.8 multiply_convert_fusion.2
  10.1 0.8 copy.71
  10.9 5.4 %all-to-all-start = ((bf16[256,1,2,128]{3,2,1,0:T(2,128)(2,1)}), bf16[256,1,2,128]{3,2,1,0:T(2,128)(2,1)S(1)}, u32[]{:S(2)}, u32[]{:S(2)}) async-start(bf16[256,1,2,128]{3,2,1,0:T(2,128)(2,1)} %copy.71), calls=%async_computation | async-start | bytes 262144 | tf_op jit(solution)/shard_map/all_to_all | solution.py:85
  16.4 4.7 %all-to-all-done = bf16[256,1,2,128]{3,2,1,0:T(2,128)(2,1)S(1)} async-done(((bf16[256,1,2,128]{3,2,1,0:T(2,128)(2,1)}), bf16[256,1,2,128]{3,2,1,0:T(2,128)(2,1)S(1)}, u32[]{:S(2)}, u32[]{:S(2)}) %all-to-all-start) | async-done | bytes 131104 | tf_op jit(solution)/shard_map/all_to_all | solution.py:85
  21.1 5.2 %collective-permute-start = (bf16[64,4,1,128]{3,0,1,2:T(8,128)(2,1)S(1)}, bf16[64,4,1,128]{3,0,1,2:T(8,128)(2,1)S(1)}, u32[]{:S(2)}, u32[]{:S(2)}) collective-permute-start(bf16[64,4,1,128]{3,0,1,2:T(8,128)(2,1)S(1)} %get-tuple-element.33), channel_id=1, source_target_pairs={{0,1},{1,2},{2,3},{4,5},{5,6},{6,7},{8,9},{9,10},{10,11},{12,13},{... | collective-permute-start | bytes 196616 | tf_op jit(solution)/shard_map/ppermute | solution.py:15
  26.4 1.9 collective-permute-start.1
  28.4 3.5 %collective-permute-done.1 = bf16[64,4,1,128]{3,0,1,2:T(8,128)(2,1)S(1)} collective-permute-done((bf16[64,4,1,128]{3,0,1,2:T(8,128)(2,1)S(1)}, bf16[64,4,1,128]{3,0,1,2:T(8,128)(2,1)S(1)}, u32[]{:S(2)}, u32[]{:S(2)}) %collective-permute-start.1) | collective-permute-done | bytes 65568 | tf_op jit(solution)/shard_map/ppermute | solution.py:18
  32.0 0.3 copy.107
  32.3 0.3 pad.5.clone
  32.7 0.3 copy-done.5
  33.0 1.2 add_multiply_fusion
  34.2 0.3 copy.76
  34.8 0.7 fusion.28
  35.5 3.3 %all-to-all-start.1 = ((bf16[64,4,2,128]{3,0,2,1:T(8,128)(2,1)}), bf16[64,4,2,128]{3,0,2,1:T(8,128)(2,1)S(1)}, u32[]{:S(2)}, u32[]{:S(2)}) async-start(bf16[64,4,2,128]{3,0,2,1:T(8,128)(2,1)} %fusion.28), calls=%async_computation.1 | async-start | bytes 262144 | tf_op jit(solution)/shard_map/all_to_all | solution.py:89
  38.9 0.8 copy.79
  39.7 0.3 copy.91
  40.2 0.2 pad_bitcast_fusion
  40.5 1.7 copy.93
  42.2 1.4 all-to-all-done.1
  43.7 1.3 fusion.24
  45.2 0.8 copy.80
  46.0 3.3 %all-to-all-start.2 = ((bf16[256,1,2,128]{3,2,1,0:T(2,128)(2,1)}), bf16[256,1,2,128]{3,2,1,0:T(2,128)(2,1)S(1)}, u32[]{:S(2)}, u32[]{:S(2)}) async-start(bf16[256,1,2,128]{3,2,1,0:T(2,128)(2,1)} %copy.80), calls=%async_computation.2 | async-start | bytes 262144 | tf_op jit(solution)/shard_map/all_to_all | solution.py:107
  49.4 0.8 copy.96
  50.1 0.9 fusion.35
  51.1 3.5 %all-to-all-done.2 = bf16[256,1,2,128]{3,2,1,0:T(2,128)(2,1)S(1)} async-done(((bf16[256,1,2,128]{3,2,1,0:T(2,128)(2,1)}), bf16[256,1,2,128]{3,2,1,0:T(2,128)(2,1)S(1)}, u32[]{:S(2)}, u32[]{:S(2)}) %all-to-all-start.2) | async-done | bytes 131104 | tf_op jit(solution)/shard_map/all_to_all | solution.py:107
  54.8 3.7 %collective-permute-start.2 = (bf16[64,4,1,128]{3,0,2,1:T(8,128)(2,1)S(1)}, bf16[64,4,1,128]{3,0,2,1:T(8,128)(2,1)S(1)}, u32[]{:S(2)}, u32[]{:S(2)}) collective-permute-start(bf16[64,4,1,128]{3,0,2,1:T(8,128)(2,1)S(1)} %get-tuple-element.31), channel_id=1, source_target_pairs={{0,1},{1,2},{2,3},{4,5},{5,6},{6,7},{8,9},{9,10},{10,11},{12,13},{... | collective-permute-start | bytes 196616 | tf_op jit(solution)/shard_map/ppermute | solution.py:15
  58.4 1.9 collective-permute-start.3
  60.4 0.4 copy.94
  60.8 3.2 %collective-permute-done.3 = bf16[64,4,1,128]{3,0,2,1:T(8,128)(2,1)S(1)} collective-permute-done((bf16[64,4,1,128]{3,0,2,1:T(8,128)(2,1)S(1)}, bf16[64,4,1,128]{3,0,2,1:T(8,128)(2,1)S(1)}, u32[]{:S(2)}, u32[]{:S(2)}) %collective-permute-start.3) | collective-permute-done | bytes 65568 | tf_op jit(solution)/shard_map/ppermute | solution.py:18
  64.1 0.3 copy.108
  64.4 0.3 pad.7.clone
  64.8 2.1 %fusion.4 = bf16[4,2,8,17,64]{4,2,3,1,0:T(8,128)(2,1)S(1)} fusion(bf16[64,4,4,1,7,2]{0,4,5,2,1,3:T(8,128)(2,1)S(1)} %slice.27, bf16[64,4,4,1,8,17]{0,4,5,2,1,3:T(8,128)(2,1)S(1)} %copy.85, pred[8,17]{0,1:T(8,128)(4,1)S(1)} %copy-done.5, bf16[64,64]{0,1:T(8,128)(2,1)S(1)} %compare_convert_fusion, bf16[64,8,3,3,3]{0,1,4,3,2:T(8,128)(2,1)S(1)} %constant_dynamic-slice_fusion), kind=kOutput, calls=%fused_computation.8 | convolution fusion | flops 202055680 | bytes 482440 | tf_op jit(solution)/shard_map/conv_general_dilated | solution.py:30
  67.3 0.8 copy.87
  68.1 3.3 %all-to-all-start.3 = ((bf16[64,4,2,128]{3,0,2,1:T(8,128)(2,1)}), bf16[64,4,2,128]{3,0,2,1:T(8,128)(2,1)S(1)}, u32[]{:S(2)}, u32[]{:S(2)}) async-start(bf16[64,4,2,128]{3,0,2,1:T(8,128)(2,1)} %copy.87), calls=%async_computation.3 | async-start | bytes 262144 | tf_op jit(solution)/shard_map/all_to_all | solution.py:114
  71.4 0.2 all-reduce.4.cloned.1.call-start
  71.7 7.9 %fusion.3 = f32[8,64,3,3,3]{1,0,4,3,2:T(8,128)S(1)} fusion(bf16[1,64,6,4,130]{1,0,4,3,2:T(2,128)(2,1)S(1)} %copy.93, bf16[1,64,4,2,128]{1,0,4,3,2:T(2,128)(2,1)S(1)} %copy.94, f32[8,64]{1,0:T(8,128)S(1)} %fusion.40), kind=kOutput, calls=%fused_computation.7 | convolution fusion | flops 226699776 | bytes 587776 | tf_op jit(solution)/shard_map/conv_general_dilated | solution.py:59
  79.6 11.5 %psum.22 = f32[64,8,3,3,3]{0,1,4,3,2:T(8,128)S(1)} all-reduce(f32[64,8,3,3,3]{0,1,4,3,2:T(8,128)S(1)} %bitcast.154), channel_id=1, replica_groups=mesh['rep'=2,'grp'=4,'sub'=4] {'sub'}, use_global_device_ids=true, to_apply=%region_2.3 | all-reduce | flops 13824 | bytes 110592 | tf_op jit(solution)/shard_map/psum | solution.py:115
  91.2 0.2 copy.101
  91.4 0.3 reshape.178
  91.9 0.9 convolution_bitcast_fusion.1
  92.9 0.7 broadcast_multiply_fusion.2
  93.5 0.2 fusion.7
  93.7 0.8 copy.97
  94.5 89.9 %all-reduce.4.cloned.1.call-done = (f32[256,256]{0,1:T(8,128)}, f32[256,256]{0,1:T(8,128)}) async-done(((f32[256,256]{0,1:T(8,128)}, f32[256,256]{0,1:T(8,128)}), (f32[256,256]{0,1:T(8,128)}, f32[256,256]{0,1:T(8,128)})) %all-reduce.4.cloned.1.call-update) | async-done | bytes 524304 | tf_op jit(solution)/shard_map/psum | solution.py:130
  184.5 1.1 broadcast_multiply_fusion
  185.5 0.8 copy.98
  186.4 0.8 copy.99
  (41 shorter events, 2.0 us)
Async XLA Ops:
  7.2 36.6 %copy-start = (bf16[256,256]{1,0:T(8,128)(2,1)S(1)}, bf16[256,256]{1,0:T(8,128)(2,1)}, u32[]{:S(2)}) copy-start(bf16[256,256]{1,0:T(8,128)(2,1)} %param.9) | copy-start | bytes 393220
  8.2 20.1 %copy-start.4 = (bf16[256,8,3,3,3]{0,1,4,3,2:T(8,128)(2,1)S(1)}, bf16[256,8,3,3,3]{0,1,4,3,2:T(8,128)(2,1)}, u32[]{:S(2)}) copy-start(bf16[256,8,3,3,3]{0,1,4,3,2:T(8,128)(2,1)} %param.8) | copy-start | bytes 331780
  10.9 10.2 %all-to-all-start = ((bf16[256,1,2,128]{3,2,1,0:T(2,128)(2,1)}), bf16[256,1,2,128]{3,2,1,0:T(2,128)(2,1)S(1)}, u32[]{:S(2)}, u32[]{:S(2)}) async-start(bf16[256,1,2,128]{3,2,1,0:T(2,128)(2,1)} %copy.71), calls=%async_computation | async-start | bytes 262144 | tf_op jit(solution)/shard_map/all_to_all | solution.py:85
  21.1 7.3 %collective-permute-start = (bf16[64,4,1,128]{3,0,1,2:T(8,128)(2,1)S(1)}, bf16[64,4,1,128]{3,0,1,2:T(8,128)(2,1)S(1)}, u32[]{:S(2)}, u32[]{:S(2)}) collective-permute-start(bf16[64,4,1,128]{3,0,1,2:T(8,128)(2,1)S(1)} %get-tuple-element.33), channel_id=1, source_target_pairs={{0,1},{1,2},{2,3},{4,5},{5,6},{6,7},{8,9},{9,10},{10,11},{12,13},{... | collective-permute-start | bytes 196616 | tf_op jit(solution)/shard_map/ppermute | solution.py:15
  26.4 5.6 %collective-permute-start.1 = (bf16[64,4,1,128]{3,0,1,2:T(8,128)(2,1)S(1)}, bf16[64,4,1,128]{3,0,1,2:T(8,128)(2,1)S(1)}, u32[]{:S(2)}, u32[]{:S(2)}) collective-permute-start(bf16[64,4,1,128]{3,0,1,2:T(8,128)(2,1)S(1)} %get-tuple-element.34), channel_id=1, source_target_pairs={{1,0},{2,1},{3,2},{5,4},{6,5},{7,6},{9,8},{10,9},{11,10},{13,12},{... | collective-permute-start | bytes 196616 | tf_op jit(solution)/shard_map/ppermute | solution.py:18
  32.3 0.7 copy-start.5
  34.5 4.3 %copy-start.2 = (bf16[256,1,2,128]{3,2,1,0:T(2,128)(2,1)S(1)}, bf16[256,1,2,128]{3,2,1,0:T(2,128)(2,1)}, u32[]{:S(2)}) copy-start(bf16[256,1,2,128]{3,2,1,0:T(2,128)(2,1)} %param.6) | copy-start | bytes 393220
  35.5 8.1 %all-to-all-start.1 = ((bf16[64,4,2,128]{3,0,2,1:T(8,128)(2,1)}), bf16[64,4,2,128]{3,0,2,1:T(8,128)(2,1)S(1)}, u32[]{:S(2)}, u32[]{:S(2)}) async-start(bf16[64,4,2,128]{3,0,2,1:T(8,128)(2,1)} %fusion.28), calls=%async_computation.1 | async-start | bytes 262144 | tf_op jit(solution)/shard_map/all_to_all | solution.py:89
  46.0 8.6 %all-to-all-start.2 = ((bf16[256,1,2,128]{3,2,1,0:T(2,128)(2,1)}), bf16[256,1,2,128]{3,2,1,0:T(2,128)(2,1)S(1)}, u32[]{:S(2)}, u32[]{:S(2)}) async-start(bf16[256,1,2,128]{3,2,1,0:T(2,128)(2,1)} %copy.80), calls=%async_computation.2 | async-start | bytes 262144 | tf_op jit(solution)/shard_map/all_to_all | solution.py:107
  54.8 6.0 %collective-permute-start.2 = (bf16[64,4,1,128]{3,0,2,1:T(8,128)(2,1)S(1)}, bf16[64,4,1,128]{3,0,2,1:T(8,128)(2,1)S(1)}, u32[]{:S(2)}, u32[]{:S(2)}) collective-permute-start(bf16[64,4,1,128]{3,0,2,1:T(8,128)(2,1)S(1)} %get-tuple-element.31), channel_id=1, source_target_pairs={{0,1},{1,2},{2,3},{4,5},{5,6},{6,7},{8,9},{9,10},{10,11},{12,13},{... | collective-permute-start | bytes 196616 | tf_op jit(solution)/shard_map/ppermute | solution.py:15
  58.4 5.6 %collective-permute-start.3 = (bf16[64,4,1,128]{3,0,2,1:T(8,128)(2,1)S(1)}, bf16[64,4,1,128]{3,0,2,1:T(8,128)(2,1)S(1)}, u32[]{:S(2)}, u32[]{:S(2)}) collective-permute-start(bf16[64,4,1,128]{3,0,2,1:T(8,128)(2,1)S(1)} %get-tuple-element.32), channel_id=1, source_target_pairs={{1,0},{2,1},{3,2},{5,4},{6,5},{7,6},{9,8},{10,9},{11,10},{13,12},{... | collective-permute-start | bytes 196616 | tf_op jit(solution)/shard_map/ppermute | solution.py:18
  68.1 23.1 %all-to-all-start.3 = ((bf16[64,4,2,128]{3,0,2,1:T(8,128)(2,1)}), bf16[64,4,2,128]{3,0,2,1:T(8,128)(2,1)S(1)}, u32[]{:S(2)}, u32[]{:S(2)}) async-start(bf16[64,4,2,128]{3,0,2,1:T(8,128)(2,1)} %copy.87), calls=%async_computation.3 | async-start | bytes 262144 | tf_op jit(solution)/shard_map/all_to_all | solution.py:114
  71.4 113.0 %all-reduce.4.cloned.1.call-start = ((), (), s32[]{:S(2)}) async-start(), calls=%async_computation.4 | async-start | bytes 1048576 | tf_op jit(solution)/shard_map/psum | solution.py:130
  79.6 12.2 %copy-start.1 = (f32[256,256]{0,1:T(8,128)S(1)}, f32[256,256]{0,1:T(8,128)}, u32[]{:S(2)}) copy-start(f32[256,256]{0,1:T(8,128)} %get-tuple-element.36) | copy-start | bytes 786436
  91.4 2.1 %copy-start.3 = (bf16[256,256]{1,0:T(8,128)(2,1)S(1)}, bf16[256,256]{1,0:T(8,128)(2,1)}, u32[]{:S(2)}) copy-start(bf16[256,256]{1,0:T(8,128)(2,1)} %param.7) | copy-start | bytes 393220
Sparse Core Ops, SparseCore 0:
  93.0 91.4 all-reduce.3
where the time goes:
time: 195 us; the launch traced here: 194 us
  waiting for transfers between devices  106 us (54%)
  starting transfers between devices  28.3 us (15%)
  matrix products  16.7 us (9%)
  between operations  14.5 us (7%)
  local copies, waits for them, and re-layouts  13.7 us (7%)
  blocking collectives  11.5 us (6%)
  other arithmetic  2.91 us (1%)
    psum x1, waiting for transfers between devices, per_device(): first_grad = lax.psum(first_part, ('grp', 'sub')) * factor  89.9 us
    psum x1, blocking collectives, per_device(): group_grad = lax.psum(kernel_part, 'sub') * factor  11.5 us
    ppermute x2, starting transfers between devices, padded_2(): lax.ppermute(lax.slice_in_dim(block, block.shape[dim] - width, None, axis...  8.89 us
    conv_general_dilated x1, matrix products, weight_grad(): lax.conv_general_dilated(padded[None], deltas[None], (1, 1, 1), 'VALID',...  7.92 us
    ppermute x2, waiting for transfers between devices, padded_2(): lax.ppermute(lax.slice_in_dim(block, 0, width, axis=dim), axis, backward)  6.74 us
    unnamed x21, local copies, waits for them, and re-layouts  5.57 us
    all_to_all x1, starting transfers between devices, per_device(): lax.all_to_all(first_act, 'grp', split_axis=0, concat_axis=1, tiled=True)  5.42 us
    all_to_all x1, waiting for transfers between devices, per_device(): lax.all_to_all(first_act, 'grp', split_axis=0, concat_axis=1, tiled=True)  4.73 us
  transfers between devices with their start and end apart: 9, of which 6 were waited for; matrix products, arithmetic and copies ran while one was open for 8% of the time, Pallas kernels for 0%

commit v1 on v0

--- a/solution.py
+++ b/solution.py
@@ -5,6 +5,12 @@
 from jax.sharding import PartitionSpec as P
 
 GW = 8
+
+
+def gather_and_add(array, name):
+    pieces = lax.all_gather(array, name, axis=0, tiled=False)
+    total = pieces.sum(axis=0)
+    return total
 
 
 def padded_2(block, sides, width):
@@ -112,7 +118,7 @@
     dense_grad = weight_grad(jnp.pad(padded_act, ((0, 0), (1, 1), (0, 0), (1, 1))), group_delta)
     kernel_part = diagonal_blocks(dense_grad)
     inner_grad = lax.all_to_all(inner_local, "grp", split_axis=1, concat_axis=0, tiled=True)
-    group_grad = lax.psum(kernel_part, "sub") * factor
+    group_grad = gather_and_add(kernel_part, "sub") * factor
     first_delta = (
         inner_grad.reshape(channels, -1).astype(jnp.float32) * silu_slope(first_pre)
     ).astype(jnp.bfloat16)

time: 195 us -> 219 us (1.12)
  blocking collectives: 11.5 us -> 28.8 us
  other arithmetic: 2.91 us -> 7.21 us
    all_gather x0 -> x1, blocking collectives: none -> 28.8 us  [gather_and_add(): pieces = lax.all_gather(array, name, axis=0, tiled=False)]
    psum x1 -> x0, blocking collectives: 11.5 us -> none  [per_device(): group_grad = lax.psum(kernel_part, 'sub') * factor]
    reduce_sum x0 -> x1, other arithmetic: none -> 3.75 us  [gather_and_add(): total = pieces.sum(axis=0)]
    unnamed x21 -> x26, local copies, waits for them, and re-layouts: 5.57 us -> 6.52 us
  transfers between devices with their start and end apart: 9 -> 9, of which waited for: 6 -> 6; matrix products, arithmetic and copies ran while one was open for 8% -> 9% of each run, Pallas kernels for 0% -> 0%
where the time goes in v1:
time: 219 us; the launch traced here: 218 us
  waiting for transfers between devices  107 us (49%)
  starting transfers between devices  29 us (13%)
  blocking collectives  28.8 us (13%)
  matrix products  16.7 us (8%)
  local copies, waits for them, and re-layouts  15.1 us (7%)
  between operations  14.5 us (7%)
  other arithmetic  7.21 us (3%)
    psum x1, waiting for transfers between devices, per_device(): first_grad = lax.psum(first_part, ('grp', 'sub')) * factor  89.5 us
    all_gather x1, blocking collectives, gather_and_add(): pieces = lax.all_gather(array, name, axis=0, tiled=False)  28.8 us
    ppermute x2, starting transfers between devices, padded_2(): lax.ppermute(lax.slice_in_dim(block, block.shape[dim] - width, None, axis...  8.89 us
    conv_general_dilated x1, matrix products, weight_grad(): lax.conv_general_dilated(padded[None], deltas[None], (1, 1, 1), 'VALID',...  7.94 us
    ppermute x2, waiting for transfers between devices, padded_2(): lax.ppermute(lax.slice_in_dim(block, 0, width, axis=dim), axis, backward)  6.74 us
    unnamed x26, local copies, waits for them, and re-layouts  6.52 us
    all_to_all x1, starting transfers between devices, per_device(): lax.all_to_all(first_act, 'grp', split_axis=0, concat_axis=1, tiled=True)  5.42 us
    all_to_all x1, waiting for transfers between devices, per_device(): lax.all_to_all(first_act, 'grp', split_axis=0, concat_axis=1, tiled=True)  4.73 us
  transfers between devices with their start and end apart: 9, of which 6 were waited for; matrix products, arithmetic and copies ran while one was open for 9% of the time, Pallas kernels for 0%

profile of v1, /device:TPU:1, one launch (start us, length us, event | category | flops | bytes accessed | tf_op | source)
XLA Modules:
  0.0 218.1 jit_solution(13073905262246154458)
XLA Ops:
  7.2 1.0 copy.129
  8.3 1.9 multiply_convert_fusion.2
  10.1 0.8 copy.130
  10.9 5.4 %all-to-all-start = ((bf16[256,1,2,128]{3,2,1,0:T(2,128)(2,1)}), bf16[256,1,2,128]{3,2,1,0:T(2,128)(2,1)S(1)}, u32[]{:S(2)}, u32[]{:S(2)}) async-start(bf16[256,1,2,128]{3,2,1,0:T(2,128)(2,1)} %copy.130), calls=%async_computation | async-start | bytes 262144 | tf_op jit(solution)/shard_map/all_to_all | solution.py:91
  16.4 4.7 %all-to-all-done = bf16[256,1,2,128]{3,2,1,0:T(2,128)(2,1)S(1)} async-done(((bf16[256,1,2,128]{3,2,1,0:T(2,128)(2,1)}), bf16[256,1,2,128]{3,2,1,0:T(2,128)(2,1)S(1)}, u32[]{:S(2)}, u32[]{:S(2)}) %all-to-all-start) | async-done | bytes 131104 | tf_op jit(solution)/shard_map/all_to_all | solution.py:91
  21.2 5.2 %collective-permute-start = (bf16[64,4,1,128]{3,0,1,2:T(8,128)(2,1)S(1)}, bf16[64,4,1,128]{3,0,1,2:T(8,128)(2,1)S(1)}, u32[]{:S(2)}, u32[]{:S(2)}) collective-permute-start(bf16[64,4,1,128]{3,0,1,2:T(8,128)(2,1)S(1)} %get-tuple-element.43), channel_id=1, source_target_pairs={{0,1},{1,2},{2,3},{4,5},{5,6},{6,7},{8,9},{9,10},{10,11},{12,13},{... | collective-permute-start | bytes 196616 | tf_op jit(solution)/shard_map/ppermute | solution.py:21
  26.4 1.9 collective-permute-start.1
  28.5 3.5 %collective-permute-done.1 = bf16[64,4,1,128]{3,0,1,2:T(8,128)(2,1)S(1)} collective-permute-done((bf16[64,4,1,128]{3,0,1,2:T(8,128)(2,1)S(1)}, bf16[64,4,1,128]{3,0,1,2:T(8,128)(2,1)S(1)}, u32[]{:S(2)}, u32[]{:S(2)}) %collective-permute-start.1) | collective-permute-done | bytes 65568 | tf_op jit(solution)/shard_map/ppermute | solution.py:24
  32.0 0.3 copy.168
  32.4 0.3 pad.5.clone
  32.8 0.3 copy-done.7
  33.0 1.2 add_multiply_fusion
  34.3 0.3 copy.135
  34.8 0.7 fusion.28
  35.6 3.3 %all-to-all-start.1 = ((bf16[64,4,2,128]{3,0,2,1:T(8,128)(2,1)}), bf16[64,4,2,128]{3,0,2,1:T(8,128)(2,1)S(1)}, u32[]{:S(2)}, u32[]{:S(2)}) async-start(bf16[64,4,2,128]{3,0,2,1:T(8,128)(2,1)} %fusion.28), calls=%async_computation.1 | async-start | bytes 262144 | tf_op jit(solution)/shard_map/all_to_all | solution.py:95
  38.9 0.8 copy.138
  39.7 0.3 copy.150
  40.5 1.7 copy.152
  42.2 1.4 all-to-all-done.1
  43.8 1.3 fusion.24
  45.1 0.8 copy.156
  46.1 0.8 copy.139
  46.9 3.3 %all-to-all-start.2 = ((bf16[256,1,2,128]{3,2,1,0:T(2,128)(2,1)}), bf16[256,1,2,128]{3,2,1,0:T(2,128)(2,1)S(1)}, u32[]{:S(2)}, u32[]{:S(2)}) async-start(bf16[256,1,2,128]{3,2,1,0:T(2,128)(2,1)} %copy.139), calls=%async_computation.2 | async-start | bytes 262144 | tf_op jit(solution)/shard_map/all_to_all | solution.py:113
  50.2 0.9 fusion.35
  51.1 4.3 %all-to-all-done.2 = bf16[256,1,2,128]{3,2,1,0:T(2,128)(2,1)S(1)} async-done(((bf16[256,1,2,128]{3,2,1,0:T(2,128)(2,1)}), bf16[256,1,2,128]{3,2,1,0:T(2,128)(2,1)S(1)}, u32[]{:S(2)}, u32[]{:S(2)}) %all-to-all-start.2) | async-done | bytes 131104 | tf_op jit(solution)/shard_map/all_to_all | solution.py:113
  55.6 3.7 %collective-permute-start.2 = (bf16[64,4,1,128]{3,0,2,1:T(8,128)(2,1)S(1)}, bf16[64,4,1,128]{3,0,2,1:T(8,128)(2,1)S(1)}, u32[]{:S(2)}, u32[]{:S(2)}) collective-permute-start(bf16[64,4,1,128]{3,0,2,1:T(8,128)(2,1)S(1)} %get-tuple-element.41), channel_id=1, source_target_pairs={{0,1},{1,2},{2,3},{4,5},{5,6},{6,7},{8,9},{9,10},{10,11},{12,13},{... | collective-permute-start | bytes 196616 | tf_op jit(solution)/shard_map/ppermute | solution.py:21
  59.3 1.9 collective-permute-start.3
  61.2 0.4 copy.153
  61.7 3.2 %collective-permute-done.3 = bf16[64,4,1,128]{3,0,2,1:T(8,128)(2,1)S(1)} collective-permute-done((bf16[64,4,1,128]{3,0,2,1:T(8,128)(2,1)S(1)}, bf16[64,4,1,128]{3,0,2,1:T(8,128)(2,1)S(1)}, u32[]{:S(2)}, u32[]{:S(2)}) %collective-permute-start.3) | collective-permute-done | bytes 65568 | tf_op jit(solution)/shard_map/ppermute | solution.py:24
  64.9 0.3 copy.169
  65.2 0.3 pad.7.clone
  65.6 2.1 fusion.4
  68.1 0.8 copy.146
  68.9 3.9 %all-to-all-start.3 = ((bf16[64,4,2,128]{3,0,2,1:T(8,128)(2,1)}), bf16[64,4,2,128]{3,0,2,1:T(8,128)(2,1)}, u32[]{:S(2)}, u32[]{:S(2)}) async-start(bf16[64,4,2,128]{3,0,2,1:T(8,128)(2,1)} %copy.146), calls=%async_computation.3 | async-start | bytes 262144 | tf_op jit(solution)/shard_map/all_to_all | solution.py:120
  73.1 7.9 %fusion.3 = f32[8,64,3,3,3]{1,0,4,3,2:T(8,128)S(1)} fusion(bf16[1,64,6,4,130]{1,0,4,3,2:T(2,128)(2,1)S(1)} %copy.152, bf16[1,64,4,2,128]{1,0,4,3,2:T(2,128)(2,1)S(1)} %copy.153, f32[8,64]{1,0:T(8,128)S(1)} %fusion.40), kind=kOutput, calls=%fused_computation.7 | convolution fusion | flops 226699776 | bytes 587776 | tf_op jit(solution)/shard_map/conv_general_dilated | solution.py:65
  81.0 0.4 copy.154
  81.5 28.8 %all-gather = f32[256,8,3,3,3]{1,4,3,2,0:T(4,128)} all-gather(f32[64,8,3,3,3]{1,4,3,2,0:T(4,128)S(1)} %copy.154), channel_id=2, replica_groups=mesh['rep'=2,'grp'=4,'sub'=4] {'sub'}, dimensions={0}, use_global_device_ids=true | all-gather | bytes 276480 | tf_op jit(solution)/shard_map/all_gather | solution.py:11
  110.3 3.7 %reduce_sum.19 = f32[64,8,3,3,3]{1,4,3,2,0:T(4,128)S(1)} reduce(f32[4,64,8,3,3,3]{2,5,4,3,1,0:T(4,128)} %bitcast.136, f32[]{:T(128)} %constant.46.clone.1), dimensions={0}, to_apply=%region_2.3 | reduce | flops 41472 | bytes 276484 | tf_op jit(solution)/shard_map/reduce_sum | solution.py:12
  114.1 1.0 convert_bitcast_fusion
  115.3 0.3 reshape.179
  115.8 0.9 convolution_bitcast_fusion.1
  116.8 0.3 broadcast_multiply_fusion
  117.0 0.9 copy.159
  118.2 0.8 copy.157
  119.0 89.5 %all-reduce.4.cloned.1.call-done = (f32[256,256]{0,1:T(8,128)}, f32[256,256]{0,1:T(8,128)}) async-done(((f32[256,256]{0,1:T(8,128)}, f32[256,256]{0,1:T(8,128)}), (f32[256,256]{0,1:T(8,128)}, f32[256,256]{0,1:T(8,128)})) %all-reduce.4.cloned.1.call-update) | async-done | bytes 524304 | tf_op jit(solution)/shard_map/psum | solution.py:136
  208.5 1.1 broadcast_multiply_fusion.1
  209.6 0.8 copy.160
  210.4 0.8 copy.158
  (48 shorter events, 2.9 us)
Async XLA Ops:
  7.2 36.6 %copy-start = (bf16[256,256]{1,0:T(8,128)(2,1)S(1)}, bf16[256,256]{1,0:T(8,128)(2,1)}, u32[]{:S(2)}) copy-start(bf16[256,256]{1,0:T(8,128)(2,1)} %param.9) | copy-start | bytes 393220
  8.2 35.5 %copy-start.1 = (bf16[256,1,2,128]{0,3,2,1:T(8,128)(2,1)}, bf16[256,1,2,128]{0,3,2,1:T(8,128)(2,1)S(1)}, u32[]{:S(2)}) copy-start(bf16[256,1,2,128]{0,3,2,1:T(8,128)(2,1)S(1)} %copy.129) | copy-start | bytes 393220
  8.2 20.1 %copy-start.6 = (bf16[256,8,3,3,3]{0,1,4,3,2:T(8,128)(2,1)S(1)}, bf16[256,8,3,3,3]{0,1,4,3,2:T(8,128)(2,1)}, u32[]{:S(2)}) copy-start(bf16[256,8,3,3,3]{0,1,4,3,2:T(8,128)(2,1)} %param.8) | copy-start | bytes 331780
  10.9 10.2 %all-to-all-start = ((bf16[256,1,2,128]{3,2,1,0:T(2,128)(2,1)}), bf16[256,1,2,128]{3,2,1,0:T(2,128)(2,1)S(1)}, u32[]{:S(2)}, u32[]{:S(2)}) async-start(bf16[256,1,2,128]{3,2,1,0:T(2,128)(2,1)} %copy.130), calls=%async_computation | async-start | bytes 262144 | tf_op jit(solution)/shard_map/all_to_all | solution.py:91
  21.2 7.3 %collective-permute-start = (bf16[64,4,1,128]{3,0,1,2:T(8,128)(2,1)S(1)}, bf16[64,4,1,128]{3,0,1,2:T(8,128)(2,1)S(1)}, u32[]{:S(2)}, u32[]{:S(2)}) collective-permute-start(bf16[64,4,1,128]{3,0,1,2:T(8,128)(2,1)S(1)} %get-tuple-element.43), channel_id=1, source_target_pairs={{0,1},{1,2},{2,3},{4,5},{5,6},{6,7},{8,9},{9,10},{10,11},{12,13},{... | collective-permute-start | bytes 196616 | tf_op jit(solution)/shard_map/ppermute | solution.py:21
  26.4 5.6 %collective-permute-start.1 = (bf16[64,4,1,128]{3,0,1,2:T(8,128)(2,1)S(1)}, bf16[64,4,1,128]{3,0,1,2:T(8,128)(2,1)S(1)}, u32[]{:S(2)}, u32[]{:S(2)}) collective-permute-start(bf16[64,4,1,128]{3,0,1,2:T(8,128)(2,1)S(1)} %get-tuple-element.44), channel_id=1, source_target_pairs={{1,0},{2,1},{3,2},{5,4},{6,5},{7,6},{9,8},{10,9},{11,10},{13,12},{... | collective-permute-start | bytes 196616 | tf_op jit(solution)/shard_map/ppermute | solution.py:24
  32.4 0.7 copy-start.7
  34.6 4.3 %copy-start.4 = (bf16[256,1,2,128]{3,2,1,0:T(2,128)(2,1)S(1)}, bf16[256,1,2,128]{3,2,1,0:T(2,128)(2,1)}, u32[]{:S(2)}) copy-start(bf16[256,1,2,128]{3,2,1,0:T(2,128)(2,1)} %param.6) | copy-start | bytes 393220
  35.6 8.1 %all-to-all-start.1 = ((bf16[64,4,2,128]{3,0,2,1:T(8,128)(2,1)}), bf16[64,4,2,128]{3,0,2,1:T(8,128)(2,1)S(1)}, u32[]{:S(2)}, u32[]{:S(2)}) async-start(bf16[64,4,2,128]{3,0,2,1:T(8,128)(2,1)} %fusion.28), calls=%async_computation.1 | async-start | bytes 262144 | tf_op jit(solution)/shard_map/all_to_all | solution.py:95
  46.9 8.6 %all-to-all-start.2 = ((bf16[256,1,2,128]{3,2,1,0:T(2,128)(2,1)}), bf16[256,1,2,128]{3,2,1,0:T(2,128)(2,1)S(1)}, u32[]{:S(2)}, u32[]{:S(2)}) async-start(bf16[256,1,2,128]{3,2,1,0:T(2,128)(2,1)} %copy.139), calls=%async_computation.2 | async-start | bytes 262144 | tf_op jit(solution)/shard_map/all_to_all | solution.py:113
  55.6 6.0 %collective-permute-start.2 = (bf16[64,4,1,128]{3,0,2,1:T(8,128)(2,1)S(1)}, bf16[64,4,1,128]{3,0,2,1:T(8,128)(2,1)S(1)}, u32[]{:S(2)}, u32[]{:S(2)}) collective-permute-start(bf16[64,4,1,128]{3,0,2,1:T(8,128)(2,1)S(1)} %get-tuple-element.41), channel_id=1, source_target_pairs={{0,1},{1,2},{2,3},{4,5},{5,6},{6,7},{8,9},{9,10},{10,11},{12,13},{... | collective-permute-start | bytes 196616 | tf_op jit(solution)/shard_map/ppermute | solution.py:21
  59.3 5.6 %collective-permute-start.3 = (bf16[64,4,1,128]{3,0,2,1:T(8,128)(2,1)S(1)}, bf16[64,4,1,128]{3,0,2,1:T(8,128)(2,1)S(1)}, u32[]{:S(2)}, u32[]{:S(2)}) collective-permute-start(bf16[64,4,1,128]{3,0,2,1:T(8,128)(2,1)S(1)} %get-tuple-element.42), channel_id=1, source_target_pairs={{1,0},{2,1},{3,2},{5,4},{6,5},{7,6},{9,8},{10,9},{11,10},{13,12},{... | collective-permute-start | bytes 196616 | tf_op jit(solution)/shard_map/ppermute | solution.py:24
  68.9 45.2 %all-to-all-start.3 = ((bf16[64,4,2,128]{3,0,2,1:T(8,128)(2,1)}), bf16[64,4,2,128]{3,0,2,1:T(8,128)(2,1)}, u32[]{:S(2)}, u32[]{:S(2)}) async-start(bf16[64,4,2,128]{3,0,2,1:T(8,128)(2,1)} %copy.146), calls=%async_computation.3 | async-start | bytes 262144 | tf_op jit(solution)/shard_map/all_to_all | solution.py:120
  72.9 135.6 %all-reduce.4.cloned.1.call-start = ((), (), s32[]{:S(2)}) async-start(), calls=%async_computation.4 | async-start | bytes 1048576 | tf_op jit(solution)/shard_map/psum | solution.py:136
  114.1 1.6 copy-start.3
  114.1 1.7 copy-start.2
  116.8 1.2 copy-start.5
Sparse Core Ops, SparseCore 0:
  116.9 91.5 all-reduce.3
